TPU v7x, 32 devices: a whole 2x2x4 slice. The times are simulated.
32 devices in a mesh: row: 4 (over y, core), col: 8 (over z, x).
Axes of the slice: x: 2, y: 2, z: 4, core: 2. Of those that a mesh axis runs over, the one named last changes fastest.
Arguments:
- hess: bfloat16 [10, 4, 256, 5, 8, 256], P(None, 'row', None, None, 'col'), may hold values from -6 to 6
- coupling: float32 [32, 256, 2, 256], P(('row', 'col')), may hold values from -6 to 6
- dest_row: int32 [32, 256, 1], P(('row', 'col')), may hold values from 0 to 3, as said below
- local_row: int32 [32, 256], P(('row', 'col')), may hold values from 256 to 2559
- live: int32 [32], P(('row', 'col')), may hold values from 1 to 256, 6144 in all
- pattern: int32 [40, 40], replicated, may hold values 0 or 1
Outputs:
- factor: float32 [10, 4, 256, 5, 8, 256], P(None, 'row', None, None, 'col')
Inputs may be any that keep to these rules, and one draw needn't show every extreme that they name: `dest_row`: among one owner's 256 slots, used or not, one grid row is named exactly 64 times and no grid row more than 64 times. The first live[d] slots of owner d are used; the counts sum to 6144 and one owner uses all 256.
All inputs are finite; a program needn't handle non-finite values. No bound on the sum of `live` on one device may be relied on, other than what follows from the above.
Results may differ from a plain program's by a relative error of at most 0.0003.
Values sent between devices are 32-bit elements; how exact they have to be, the bound alone decides.
No kernel may reach another device: no remote copies, remote signals or barrier semaphores. Data moves between devices by JAX's collectives and lax.ppermute only.
A program may use at most 192 MiB of HBM per device.

v0:
```python
import jax
import jax.numpy as jnp
from jax import lax
from jax.sharding import PartitionSpec as P


def broadcast(value, axis, source):
    kept = jnp.where(lax.axis_index(axis) == source, value, 0).astype(value.dtype)
    return lax.psum(kept, axis)


def symmetric(block):
    return jnp.tril(block) + jnp.swapaxes(jnp.tril(block, -1), -1, -2)


def right_solve(rows, lower_factor):
    return jax.scipy.linalg.solve_triangular(lower_factor, rows.T, lower=True).T


def leading(block00, block10, block11, link):
    size = block00.shape[0]
    first = symmetric(block00)
    second = symmetric(block11)
    coupled = link * block10
    whole = jnp.concatenate(
        [jnp.concatenate([first, coupled.T], 1), jnp.concatenate([coupled, second], 1)], 0
    )
    ident = jnp.eye(2 * size, dtype=whole.dtype)
    spread = jnp.sum(jnp.abs(whole), axis=1) - jnp.abs(jnp.diagonal(whole))
    whole = whole * (1.0 - ident) + ident * (1.0 + spread)[:, None]
    factor00 = jnp.linalg.cholesky(whole[:size, :size])
    factor10 = right_solve(whole[size:, :size], factor00)
    reduced = whole[size:, size:] - jnp.dot(factor10, factor10.T, precision=lax.Precision.HIGHEST)
    factor11 = jnp.linalg.cholesky(reduced)
    return (factor00, factor10, factor11)


def solve_rows(rows, lower_factor):
    result = right_solve(rows, lower_factor)
    return result


def panel_solve(block_rows, f00, f10, f11):
    first = solve_rows(block_rows[:, 0], f00)
    second = solve_rows(
        block_rows[:, 1] - jnp.dot(first, f10.T, precision=lax.Precision.HIGHEST), f11
    )
    return jnp.stack([first, second], 1)


def shards(hess, coupling, dest_row, local_row, live, pattern):
    grid_rows = lax.axis_size("row")
    grid_cols = lax.axis_size("col")
    here_row = lax.axis_index("row")
    here_col = lax.axis_index("col")
    row_blocks = hess.shape[0]
    col_blocks = hess.shape[3]
    block = hess.shape[2]
    slot_count = coupling.shape[1]
    bucket = slot_count // 4
    height = row_blocks * block
    mask = pattern.astype(jnp.float32)
    grid_ids = jnp.arange(grid_rows, dtype=jnp.int32)
    dest = dest_row[0, :, 0]
    active = jnp.arange(slot_count, dtype=jnp.int32) < live[0]
    hits = (dest[:, None] == grid_ids[None, :]) & active[:, None]
    ranks = jnp.cumsum(hits.astype(jnp.int32), axis=0) - 1
    place = jnp.sum(jnp.where(hits, ranks + grid_ids[None, :] * bucket, 0), axis=1)
    place = jnp.where(active, place, grid_rows * bucket)
    outgoing = (
        jnp.zeros((grid_rows * bucket, 2, block), jnp.float32)
        .at[place]
        .set(coupling[0], mode="drop")
    )
    labels = (
        jnp.zeros((grid_rows * bucket,), jnp.float32)
        .at[place]
        .set(local_row[0].astype(jnp.float32), mode="drop")
    )
    arrived, arrived_rows = (
        lax.all_to_all(
            outgoing.reshape(grid_rows, bucket, 2, block),
            "row",
            split_axis=0,
            concat_axis=0,
            tiled=True,
        ),
        lax.all_to_all(
            labels.reshape(grid_rows, bucket), "row", split_axis=0, concat_axis=0, tiled=True
        ),
    )
    partial_value = (
        jnp.zeros((height, 2, block), jnp.float32)
        .at[arrived_rows.astype(jnp.int32).reshape(-1)]
        .add(arrived.reshape(-1, 2, block))
    )
    own = hess[:, 0, :, 0, 0, :].astype(jnp.float32).reshape(height, block)
    which = (jnp.arange(2, dtype=jnp.int32) == here_col).astype(jnp.float32)
    partial_value = partial_value + own[:, None, :] * which[None, :, None]
    corner = hess[0, 0, :, 0, 0, :].astype(jnp.float32)
    at_first = ((here_row == 0) & (here_col == 0)).astype(jnp.float32)
    at_below = ((here_row == 1) & (here_col == 0)).astype(jnp.float32)
    at_second = ((here_row == 1) & (here_col == 1)).astype(jnp.float32)
    pivots = lax.psum(
        jnp.stack([at_first * corner, at_below * corner, at_second * corner]), ("row", "col")
    )
    f00, f10, f11 = leading(pivots[0], pivots[1], pivots[2], mask[1, 0])
    mine = lax.dynamic_index_in_dim(
        mask.reshape(row_blocks, grid_rows, -1), here_row, 1, keepdims=False
    )
    rowmask = jnp.repeat(mine[:, :2], block, axis=0)
    summed = lax.psum(partial_value, "col")
    panel = panel_solve(summed * rowmask[:, :, None], f00, f10, f11)
    head_first = jnp.where(here_row == 0, f00, f10)
    head_second = jnp.where(here_row == 0, jnp.zeros_like(f11), f11)
    head = jnp.stack([head_first, head_second], 1)
    panel = panel.at[:block].set(jnp.where(here_row < 2, head, panel[:block]))
    ratio = grid_cols // grid_rows
    picked = lax.dynamic_index_in_dim(
        panel.reshape(col_blocks, ratio, block, 2, block), here_col // grid_rows, 1, keepdims=False
    )
    across = broadcast(picked, "row", here_col % grid_rows)
    left = panel.reshape(height, 2 * block)
    right = across.reshape(col_blocks * block, 2 * block)
    update = jnp.dot(left, right.T, precision=lax.Precision.HIGHEST).reshape(
        row_blocks, block, col_blocks, block
    )
    tiles = jnp.transpose(hess[:, 0, :, :, 0, :].astype(jnp.float32), (0, 2, 1, 3))
    sym = symmetric(tiles)
    block_i = jnp.arange(row_blocks, dtype=jnp.int32) * grid_rows + here_row
    block_j = jnp.arange(col_blocks, dtype=jnp.int32) * grid_cols + here_col
    links = lax.dynamic_index_in_dim(
        lax.dynamic_index_in_dim(
            mask.reshape(row_blocks, grid_rows, col_blocks, grid_cols), here_row, 1, keepdims=False
        ),
        here_col,
        2,
        keepdims=False,
    )
    same = (block_i[:, None] == block_j[None, :])[:, :, None, None]
    below = (block_i[:, None] > block_j[None, :])[:, :, None, None]
    base = jnp.where(same, sym, jnp.where(below, links[:, :, None, None] * tiles, 0.0))
    trail = base - jnp.transpose(update, (0, 2, 1, 3))
    lower_panel = jnp.transpose(panel.reshape(row_blocks, block, 2, block), (0, 2, 1, 3))
    panel_tile = lax.dynamic_index_in_dim(lower_panel, jnp.minimum(here_col, 1), 1, keepdims=False)
    in_panel = (block_j < 2)[None, :, None, None]
    kept = (block_i[:, None] >= block_j[None, :])[:, :, None, None]
    result = jnp.where(in_panel, panel_tile[:, None], jnp.where(kept, trail, 0.0))
    return jnp.transpose(result, (0, 2, 1, 3)).reshape(row_blocks, 1, block, col_blocks, 1, block)


def solution(mesh):
    return jax.shard_map(
        shards,
        mesh=mesh,
        in_specs=(
            P(None, "row", None, None, "col", None),
            P(("row", "col"), None, None, None),
            P(("row", "col"), None, None),
            P(("row", "col"), None),
            P(("row", "col")),
            P(),
        ),
        out_specs=P(None, "row", None, None, "col", None),
        check_vma=False,
    )
```

profile of v0, /device:TPU:0, one launch (start us, length us, event | category | flops | bytes accessed | tf_op | source)
XLA Modules:
  0.0 492.9 jit_solution(16189000699029080055)
XLA Ops:
  7.2 0.7 and_convert_fusion
  7.9 1.2 reduce-window.6
  9.5 0.7 convert_element_type.94
  10.2 0.8 fusion.47
  11.0 1.4 scatter_custom_fusion
  13.0 4.3 all-to-all-start
  17.2 1.0 fusion.18
  18.2 0.9 pad_maximum_fusion.3
  19.1 9.4 %copy.100 = bf16[10,1,256,5,1,256]{2,5,3,0,4,1:T(8,128)(2,1)} copy(bf16[10,1,256,5,1,256]{5,2,4,3,1,0:T(8,128)(2,1)} %param.11) | data formatting | bytes 13107200 | tf_op args[0]
  28.6 2.5 slice.121
  31.8 1.5 bitcast_convert_fusion
  33.5 4.2 broadcast_multiply_fusion.1
  37.9 0.8 copy.99
  38.7 0.9 broadcast_in_dim.117
  39.7 24.2 %scatter_fusion = f32[256,2,256]{2,1,0:T(2,128)} fusion(f32[256,2,256]{2,1,0:T(2,128)} %broadcast_in_dim.117, s32[256]{0:T(256)S(1)} %bitcast.222, f32[256,2,256]{2,1,0:T(2,128)S(1)} %bitcast.212), kind=kCustom, calls=%fused_computation.2 | custom fusion | bytes 1573888 | tf_op jit(solution)/shard_map/scatter | solution.py:73
  63.8 3.5 all-to-all-start.1
  67.5 8.7 %all-to-all-done.1 = f32[4,64,2,256]{3,2,1,0:T(2,128)S(1)} async-done(((f32[4,64,2,256]{3,2,1,0:T(2,128)}), f32[4,64,2,256]{3,2,1,0:T(2,128)S(1)}, u32[]{:S(2)}, u32[]{:S(2)}) %all-to-all-start.1) | async-done | bytes 524320 | tf_op jit(solution)/shard_map/all_to_all | solution.py:81
  76.2 30.9 %scatter_fusion.1 = f32[2560,2,256]{2,1,0:T(2,128)} fusion(f32[2560,2,256]{2,1,0:T(2,128)} %broadcast_multiply_fusion.1, s32[256]{0:T(256)S(1)} %bitcast.223, f32[256,2,256]{2,1,0:T(2,128)S(1)} %bitcast.211), kind=kCustom, calls=%fused_computation.3 | custom fusion | flops 131072 | bytes 1573888 | tf_op jit(solution)/shard_map/scatter-add | solution.py:95
  107.1 8.8 %copy.88 = f32[2560,2,256]{0,2,1:T(8,128)} copy(f32[2560,2,256]{2,1,0:T(2,128)} %scatter_fusion.1) | data formatting | bytes 10485760 | tf_op jit(solution)/shard_map/scatter-add | solution.py:95
  116.1 39.1 %all-reduce.5.cloned.1.call-done = f32[3,256,256]{2,1,0:T(8,128)} async-done(((f32[3,256,256]{2,1,0:T(8,128)}), f32[3,256,256]{2,1,0:T(8,128)}) %all-reduce.5.cloned.1.call-update) | async-done | bytes 786448 | tf_op jit(solution)/shard_map/psum | solution.py:104
  155.2 1.1 fusion.26
  156.6 1.7 fusion.29
  158.8 4.5 gather_fusion
  163.8 11.7 %cholesky.130 = f32[128,128]{1,0:T(8,128)S(1)} custom-call(f32[128,128]{1,0:T(8,128)S(1)} %cholesky.194), custom_call_target="Cholesky" | custom-call | tf_op jit(solution)/shard_map/jit(cholesky)/cholesky | solution.py:31
  175.5 9.8 %custom-call.20 = f32[1,128,128]{1,2,0:T(8,128)S(1)} custom-call(f32[1,128,128]{2,1,0:T(8,128)S(1)} %get-tuple-element.87), custom_call_target="InvertDiagBlocksLowerTriangular" | custom-call | tf_op jit(solution)/shard_map/jit(cholesky)/cholesky | solution.py:31
  185.8 11.7 %cholesky.147 = f32[128,128]{1,0:T(8,128)S(1)} custom-call(f32[128,128]{1,0:T(8,128)S(1)} %convolution_subtract_fusion.6), custom_call_target="Cholesky" | custom-call | tf_op jit(solution)/shard_map/jit(cholesky)/cholesky | solution.py:31
  199.6 3.8 while.6
  200.2 1.3 bitcast_dynamic-update-slice_fusion.4
  202.1 1.3 bitcast_dynamic-update-slice_fusion.4
  203.4 20.1 %custom-call.21 = f32[2,128,128]{1,2,0:T(8,128)S(1)} custom-call(f32[2,128,128]{2,1,0:T(8,128)S(1)} %get-tuple-element.41), custom_call_target="InvertDiagBlocksLowerTriangular" | custom-call | tf_op jit(solution)/shard_map/jit(_solve_triangular)/triangular_solve | solution.py:17
  225.2 11.7 %cholesky.164 = f32[128,128]{1,0:T(8,128)S(1)} custom-call(f32[128,128]{1,0:T(8,128)S(1)} %cholesky.197), custom_call_target="Cholesky" | custom-call | tf_op jit(solution)/shard_map/jit(cholesky)/cholesky | solution.py:34
  237.0 9.8 %custom-call.22 = f32[1,128,128]{1,2,0:T(8,128)S(1)} custom-call(f32[1,128,128]{2,1,0:T(8,128)S(1)} %get-tuple-element.83), custom_call_target="InvertDiagBlocksLowerTriangular" | custom-call | tf_op jit(solution)/shard_map/jit(cholesky)/cholesky | solution.py:34
  247.3 11.7 %cholesky.181 = f32[128,128]{1,0:T(8,128)S(1)} custom-call(f32[128,128]{1,0:T(8,128)S(1)} %convolution_subtract_fusion.5), custom_call_target="Cholesky" | custom-call | tf_op jit(solution)/shard_map/jit(cholesky)/cholesky | solution.py:34
  261.5 0.8 select_bitcast_fusion
  262.3 3.8 while.7
  262.9 1.3 bitcast_dynamic-update-slice_fusion.5
  264.8 1.3 bitcast_dynamic-update-slice_fusion.5
  266.1 20.5 %custom-call.23 = f32[2,128,128]{1,2,0:T(8,128)} custom-call(f32[2,128,128]{2,1,0:T(8,128)S(1)} %get-tuple-element.42), custom_call_target="InvertDiagBlocksLowerTriangular" | custom-call | tf_op jit(solution)/shard_map/jit(_solve_triangular)/triangular_solve | solution.py:17
  286.6 0.7 fusion.21
  287.3 54.9 %all-reduce.7.cloned.1.call-done = f32[2560,2,256]{0,2,1:T(8,128)} async-done(((f32[2560,2,256]{0,2,1:T(8,128)}), f32[2560,2,256]{0,2,1:T(8,128)}) %all-reduce.7.cloned.1.call-update) | async-done | bytes 5242896 | tf_op jit(solution)/shard_map/psum | solution.py:112
  342.2 3.0 broadcast_multiply_fusion
  345.4 2.2 copy-done.1
  347.6 1.3 fusion.13
  348.8 2.3 convolution_subtract_fusion.2
  351.6 3.5 fusion.42
  355.1 4.4 fusion.8
  359.6 1.3 fusion.11
  360.8 1.1 copy-done.2
  361.9 2.3 convolution_subtract_fusion.1
  364.2 2.8 copy.97
  367.2 1.1 copy-done.4
  368.4 2.4 fusion.34
  372.3 2.2 copy-done
  374.5 2.0 copy.107
  376.5 3.2 dot_general.16
  379.8 0.8 copy-done.9
  380.6 11.4 %convert_multiply_fusion = (f32[10,256,5,256]{1,3,2,0:T(8,128)}, f32[10,256,5,256]{1,3,2,0:T(8,128)}) fusion(bf16[10,1,256,5,1,256]{2,5,3,0,4,1:T(8,128)(2,1)} %copy.100, f32[10,5]{1,0:T(8,128)S(1)} %bitcast.215, pred[256,256]{0,1:T(8,128)(4,1)S(1)} %copy-done.9), kind=kLoop, calls=%fused_computation.8 | loop fusion | flops 9830400 | bytes 32833736 | tf_op jit(solution)/shard_map/mul | solution.py:142
  392.0 14.0 %copy.102 = f32[10,256,5,256]{3,1,2,0:T(8,128)} copy(f32[10,256,5,256]{1,3,2,0:T(8,128)} %get-tuple-element.67) | data formatting | bytes 26214400 | tf_op jit(solution)/shard_map/jit(tril)/select_n | solution.py:13
  406.0 14.1 %copy.105 = f32[10,256,5,256]{3,1,2,0:T(8,128)} copy(f32[10,256,5,256]{1,3,2,0:T(8,128)} %get-tuple-element.66) | data formatting | bytes 26214400 | tf_op jit(solution)/shard_map/mul | solution.py:142
  420.3 10.4 %copy.106 = f32[2560,2,256]{2,1,0:T(2,128)} copy(f32[2560,2,256]{2,0,1:T(8,128)} %copy-done) | data formatting | bytes 10485760 | tf_op jit(solution)/shard_map/scatter | solution.py:117
  430.7 8.0 %reshape.409 = f32[10,256,512,1]{2,1,0,3:T(8,128)} reshape(f32[2560,2,256]{2,1,0:T(2,128)} %copy.106) | data formatting | bytes 10485760 | tf_op jit(solution)/shard_map/dot_general | solution.py:125
  438.7 2.0 dynamic-slice_bitcast_fusion
  440.8 30.4 %fusion.6 = f32[10,1,256,5,1,256]{5,2,3,0,4,1:T(8,128)S(1)} fusion(f32[10,256,5,256]{3,1,2,0:T(8,128)} %copy.102, f32[10,256,5,256]{3,1,2,0:T(8,128)} %copy.105, bf16[10,1,256,5,1,256]{2,5,3,0,4,1:T(8,128)(2,1)} %copy.100, f32[10,256,256]{2,1,0:T(8,128)S(1)} %dynamic-slice_bitcast_fusion, pred[5]{0:T(512)(128)(4,1)S(1)} %broadcast_compare_fusion.3, ...), kind=kOutput, calls=%fused_computation.17 | convolution fusion | flops 20158873600 | bytes 56426652 | tf_op jit(solution)/shard_map/dot_general | solution.py:125
  471.2 15.0 %copy.108 = f32[10,1,256,5,1,256]{5,4,3,2,1,0:T(1,128)} copy(f32[10,1,256,5,1,256]{5,2,3,0,4,1:T(8,128)S(1)} %fusion.6) | data formatting | bytes 26214400 | tf_op jit(solution)/shard_map/reshape | solution.py:149
  (112 shorter events, 13.2 us)
Async XLA Ops:
  13.0 50.9 %all-to-all-start = ((f32[4,1,64]{2,1,0:T(1,128)}), f32[4,1,64]{2,1,0:T(1,128)S(1)}, u32[]{:S(2)}, u32[]{:S(2)}) async-start(f32[4,1,64]{2,1,0:T(1,128)} %all_to_all.9), calls=%async_computation | async-start | bytes 4096 | tf_op jit(solution)/shard_map/all_to_all | solution.py:88
  17.2 138.0 %all-reduce.5.cloned.1.call-start = ((), (), s32[]{:S(2)}) async-start(), calls=%async_computation.2 | async-start | bytes 1572864 | tf_op jit(solution)/shard_map/psum | solution.py:104
  28.6 2.5 copy-start.11
  33.5 6.2 %copy-start.8 = (f32[1,256,2,256]{3,2,1,0:T(2,128)S(1)}, f32[1,256,2,256]{3,2,1,0:T(2,128)}, u32[]{:S(2)}) copy-start(f32[1,256,2,256]{3,2,1,0:T(2,128)} %param.12) | copy-start | bytes 1572868
  63.8 12.3 %all-to-all-start.1 = ((f32[4,64,2,256]{3,2,1,0:T(2,128)}), f32[4,64,2,256]{3,2,1,0:T(2,128)S(1)}, u32[]{:S(2)}, u32[]{:S(2)}) async-start(f32[4,64,2,256]{3,2,1,0:T(2,128)} %bitcast.26), calls=%async_computation.1 | async-start | bytes 1048576 | tf_op jit(solution)/shard_map/all_to_all | solution.py:81
  67.4 274.8 %all-reduce.7.cloned.1.call-start = ((), (), s32[]{:S(2)}) async-start(), calls=%async_computation.3 | async-start | bytes 10485760 | tf_op jit(solution)/shard_map/psum | solution.py:112
  115.9 324.9 %all-reduce.9.cloned.1.call-start = ((), (), s32[]{:S(2)}) async-start(), calls=%async_computation.4 | async-start | bytes 5242880 | tf_op jit(solution)/shard_map/psum | solution.py:9
  155.2 3.2 copy-start.5
  345.2 2.4 copy-start.1
  355.1 4.4 copy-start.10
  360.8 1.1 copy-start.2
  367.0 1.3 copy-start.4
  368.4 2.4 copy-start.3
  371.0 1.0 copy-start.6
  371.0 1.0 copy-start.7
  372.1 2.4 copy-start
  379.7 0.8 copy-start.9
Sparse Core Ops, SparseCore 0:
  23.2 131.9 all-reduce.4
  158.9 183.2 all-reduce.6
  379.9 58.9 all-reduce.8
where the time goes:
time: 500 us; the launch traced here: 493 us
  other arithmetic  172 us (34%)
  local copies, waits for them, and re-layouts  143 us (29%)
  waiting for transfers between devices  103 us (21%)
  matrix products  50.3 us (10%)
  between operations  17 us (3%)
  starting transfers between devices  8.02 us (2%)
    psum x1, waiting for transfers between devices, shards(): summed = lax.psum(partial_value, 'col')  54.9 us
    another operation x5, other arithmetic, right_solve(): return jax.scipy.linalg.solve_triangular(lower_factor, rows.T, lower=True).T  40.6 us
    psum x1, waiting for transfers between devices, shards(): lax.psum(jnp.stack([at_first * corner, at_below * corner, at_second * cor...  39.1 us
    another operation x7, other arithmetic, leading(): factor11 = jnp.linalg.cholesky(reduced)  34.6 us
    another operation x6, other arithmetic, leading(): factor00 = jnp.linalg.cholesky(whole[:size, :size])  33.9 us
    scatter-add x1, other arithmetic, shards(): partial_value = jnp.zeros((height, 2, block), jnp.float32).at[arrived_row...  30.9 us
    dot_general x1, matrix products, shards(): jnp.dot(left, right.T, precision=lax.Precision.HIGHEST)  30.4 us
    scatter x1, local copies, waits for them, and re-layouts, shards(): outgoing = jnp.zeros((grid_rows * bucket, 2, block), jnp.float32).at[plac...  24.2 us
  transfers between devices with their start and end apart: 5, of which 3 were waited for; matrix products, arithmetic and copies ran while one was open for 56% of the time, Pallas kernels for 0%

commit v1 on v0

--- a/solution.py
+++ b/solution.py
@@ -109,7 +109,9 @@
         mask.reshape(row_blocks, grid_rows, -1), here_row, 1, keepdims=False
     )
     rowmask = jnp.repeat(mine[:, :2], block, axis=0)
-    summed = lax.psum(partial_value, "col")
+    summed = partial_value
+    for hop in (1, 2, 4):
+        summed = summed + lax.ppermute(summed, "col", [(dev, dev ^ hop) for dev in range(8)])
     panel = panel_solve(summed * rowmask[:, :, None], f00, f10, f11)
     head_first = jnp.where(here_row == 0, f00, f10)
     head_second = jnp.where(here_row == 0, jnp.zeros_like(f11), f11)

time: 500 us -> 755 us (1.51)
  waiting for transfers between devices: 103 us -> 337 us
  other arithmetic: 172 us -> 186 us
    ppermute x0 -> x3, waiting for transfers between devices: none -> 214 us  [shards(): lax.ppermute(summed, 'col', [(dev, dev ^ hop) for dev in range(8)])]
    psum x1, waiting for transfers between devices: 39.1 us -> 118 us  [shards(): lax.psum(jnp.stack([at_first * corner, at_below * corner, at_second * cor...]
    psum x1 -> x0, waiting for transfers between devices: 54.9 us -> none  [shards(): summed = lax.psum(partial_value, 'col')]
    add x0 -> x2, other arithmetic: none -> 13.1 us  [shards(): summed + lax.ppermute(summed, 'col', [(dev, dev ^ hop) for dev in range(8)])]
    unnamed x28 -> x30, local copies, waits for them, and re-layouts: 17.6 us -> 17.9 us
  transfers between devices with their start and end apart: 5 -> 7, of which waited for: 3 -> 4; matrix products, arithmetic and copies ran while one was open for 56% -> 31% of each run, Pallas kernels for 0% -> 0%
where the time goes in v1:
time: 755 us; the launch traced here: 747 us
  waiting for transfers between devices  337 us (45%)
  other arithmetic  186 us (25%)
  local copies, waits for them, and re-layouts  143 us (19%)
  matrix products  50.7 us (7%)
  between operations  17.8 us (2%)
  starting transfers between devices  11.9 us (2%)
    ppermute x3, waiting for transfers between devices, shards(): lax.ppermute(summed, 'col', [(dev, dev ^ hop) for dev in range(8)])  214 us
    psum x1, waiting for transfers between devices, shards(): lax.psum(jnp.stack([at_first * corner, at_below * corner, at_second * cor...  118 us
    another operation x5, other arithmetic, right_solve(): return jax.scipy.linalg.solve_triangular(lower_factor, rows.T, lower=True).T  40.7 us
    another operation x7, other arithmetic, leading(): factor11 = jnp.linalg.cholesky(reduced)  34.6 us
    another operation x6, other arithmetic, leading(): factor00 = jnp.linalg.cholesky(whole[:size, :size])  34 us
    scatter-add x1, other arithmetic, shards(): partial_value = jnp.zeros((height, 2, block), jnp.float32).at[arrived_row...  30.9 us
    dot_general x1, matrix products, shards(): jnp.dot(left, right.T, precision=lax.Precision.HIGHEST)  30.4 us
    scatter x1, local copies, waits for them, and re-layouts, shards(): outgoing = jnp.zeros((grid_rows * bucket, 2, block), jnp.float32).at[plac...  24.2 us
  transfers between devices with their start and end apart: 7, of which 4 were waited for; matrix products, arithmetic and copies ran while one was open for 31% of the time, Pallas kernels for 0%

profile of v1, /device:TPU:0, one launch (start us, length us, event | category | flops | bytes accessed | tf_op | source)
XLA Modules:
  0.0 746.5 jit_solution(15402469535359623760)
XLA Ops:
  7.9 1.2 reduce-window.6
  11.0 1.4 scatter_custom_fusion
  13.0 4.3 all-to-all-start
  17.3 1.3 slice-done
  18.9 0.9 broadcast_in_dim.117
  19.8 24.2 %scatter_fusion = f32[256,2,256]{2,1,0:T(2,128)} fusion(f32[256,2,256]{2,1,0:T(2,128)} %broadcast_in_dim.117, s32[256]{0:T(256)S(1)} %bitcast.223, f32[256,2,256]{2,1,0:T(2,128)S(1)} %bitcast.213), kind=kCustom, calls=%fused_computation.2 | custom fusion | bytes 1573888 | tf_op jit(solution)/shard_map/scatter | solution.py:73
  44.0 3.5 all-to-all-start.1
  47.5 4.2 broadcast_multiply_fusion
  51.9 4.5 all-to-all-done.1
  56.3 30.9 %scatter_fusion.1 = f32[2560,2,256]{2,1,0:T(2,128)} fusion(f32[2560,2,256]{2,1,0:T(2,128)} %broadcast_multiply_fusion, s32[256]{0:T(256)S(1)} %bitcast.224, f32[256,2,256]{2,1,0:T(2,128)S(1)} %bitcast.212), kind=kCustom, calls=%fused_computation.3 | custom fusion | flops 131072 | bytes 1573888 | tf_op jit(solution)/shard_map/scatter-add | solution.py:95
  87.2 8.8 %copy.91 = f32[2560,2,256]{0,2,1:T(8,128)} copy(f32[2560,2,256]{2,1,0:T(2,128)} %scatter_fusion.1) | data formatting | bytes 10485760 | tf_op jit(solution)/shard_map/scatter-add | solution.py:95
  96.0 0.9 collective-permute-start
  96.9 113.3 %collective-permute-done = f32[2560,2,256]{0,2,1:T(8,128)S(1)} collective-permute-done((f32[2560,2,256]{0,2,1:T(8,128)}, f32[2560,2,256]{0,2,1:T(8,128)S(1)}, u32[]{:S(2)}, u32[]{:S(2)}) %collective-permute-start) | collective-permute-done | bytes 5242912 | tf_op jit(solution)/shard_map/ppermute | solution.py:114
  210.2 5.8 add.191
  216.0 1.7 collective-permute-start.1
  217.7 1.0 fusion.21
  218.7 0.9 pad_maximum_fusion.5
  219.7 9.5 %copy.103 = bf16[10,1,256,5,1,256]{2,5,3,0,4,1:T(8,128)(2,1)} copy(bf16[10,1,256,5,1,256]{5,2,4,3,1,0:T(8,128)(2,1)} %param.11) | data formatting | bytes 13107200 | tf_op args[0]
  230.3 0.8 copy.102
  231.2 118.1 %all-reduce.4.cloned.1.call-done = f32[3,256,256]{2,1,0:T(8,128)} async-done(((f32[3,256,256]{2,1,0:T(8,128)}), f32[3,256,256]{2,1,0:T(8,128)}) %all-reduce.4.cloned.1.call-update) | async-done | bytes 786448 | tf_op jit(solution)/shard_map/psum | solution.py:104
  349.3 1.1 fusion.29
  350.7 1.7 fusion.32
  352.9 4.8 gather_fusion
  358.0 7.4 add.192
  365.3 1.4 collective-permute-start.2
  366.8 11.7 %cholesky.130 = f32[128,128]{1,0:T(8,128)S(1)} custom-call(f32[128,128]{1,0:T(8,128)S(1)} %cholesky.194), custom_call_target="Cholesky" | custom-call | tf_op jit(solution)/shard_map/jit(cholesky)/cholesky | solution.py:31
  378.6 9.8 %custom-call.20 = f32[1,128,128]{1,2,0:T(8,128)S(1)} custom-call(f32[1,128,128]{2,1,0:T(8,128)S(1)} %get-tuple-element.87), custom_call_target="InvertDiagBlocksLowerTriangular" | custom-call | tf_op jit(solution)/shard_map/jit(cholesky)/cholesky | solution.py:31
  388.9 11.7 %cholesky.147 = f32[128,128]{1,0:T(8,128)S(1)} custom-call(f32[128,128]{1,0:T(8,128)S(1)} %convolution_subtract_fusion.4), custom_call_target="Cholesky" | custom-call | tf_op jit(solution)/shard_map/jit(cholesky)/cholesky | solution.py:31
  402.8 4.3 while.6
  403.5 1.4 bitcast_dynamic-update-slice_fusion.4
  405.6 1.4 bitcast_dynamic-update-slice_fusion.4
  407.1 20.1 %custom-call.21 = f32[2,128,128]{1,2,0:T(8,128)S(1)} custom-call(f32[2,128,128]{2,1,0:T(8,128)S(1)} %get-tuple-element.41), custom_call_target="InvertDiagBlocksLowerTriangular" | custom-call | tf_op jit(solution)/shard_map/jit(_solve_triangular)/triangular_solve | solution.py:17
  428.9 11.7 %cholesky.164 = f32[128,128]{1,0:T(8,128)S(1)} custom-call(f32[128,128]{1,0:T(8,128)S(1)} %cholesky.197), custom_call_target="Cholesky" | custom-call | tf_op jit(solution)/shard_map/jit(cholesky)/cholesky | solution.py:34
  440.7 9.8 %custom-call.22 = f32[1,128,128]{1,2,0:T(8,128)S(1)} custom-call(f32[1,128,128]{2,1,0:T(8,128)S(1)} %get-tuple-element.83), custom_call_target="InvertDiagBlocksLowerTriangular" | custom-call | tf_op jit(solution)/shard_map/jit(cholesky)/cholesky | solution.py:34
  451.0 11.7 %cholesky.181 = f32[128,128]{1,0:T(8,128)S(1)} custom-call(f32[128,128]{1,0:T(8,128)S(1)} %convolution_subtract_fusion.3), custom_call_target="Cholesky" | custom-call | tf_op jit(solution)/shard_map/jit(cholesky)/cholesky | solution.py:34
  466.2 4.0 while.7
  466.8 1.4 bitcast_dynamic-update-slice_fusion.5
  468.8 1.4 bitcast_dynamic-update-slice_fusion.5
  470.2 20.5 %custom-call.23 = f32[2,128,128]{1,2,0:T(8,128)} custom-call(f32[2,128,128]{2,1,0:T(8,128)S(1)} %get-tuple-element.42), custom_call_target="InvertDiagBlocksLowerTriangular" | custom-call | tf_op jit(solution)/shard_map/jit(_solve_triangular)/triangular_solve | solution.py:17
  491.4 101.1 %collective-permute-done.2 = f32[2560,2,256]{0,2,1:T(8,128)} collective-permute-done((f32[2560,2,256]{0,2,1:T(8,128)}, f32[2560,2,256]{0,2,1:T(8,128)}, u32[]{:S(2)}, u32[]{:S(2)}) %collective-permute-start.2) | collective-permute-done | bytes 5242912 | tf_op jit(solution)/shard_map/ppermute | solution.py:114
  592.5 5.1 add_multiply_fusion
  597.9 2.2 copy-done.1
  600.0 1.3 fusion.16
  601.5 2.3 fusion.46
  604.3 3.9 fusion.15
  608.2 4.4 fusion.9
  612.7 1.3 fusion.13
  613.9 1.1 copy-done.2
  615.0 2.3 convolution_subtract_fusion
  617.3 2.8 copy.100
  620.3 1.1 copy-done.5
  621.4 2.4 fusion.37
  625.4 2.2 copy-done
  627.6 2.0 copy.110
  629.6 3.2 dot_general.16
  632.9 0.8 copy-done.10
  633.7 11.4 %convert_multiply_fusion = (f32[10,256,5,256]{1,3,2,0:T(8,128)}, f32[10,256,5,256]{1,3,2,0:T(8,128)}) fusion(bf16[10,1,256,5,1,256]{2,5,3,0,4,1:T(8,128)(2,1)} %copy.103, f32[10,5]{1,0:T(8,128)S(1)} %bitcast.216, pred[256,256]{0,1:T(8,128)(4,1)S(1)} %copy-done.10), kind=kLoop, calls=%fused_computation.8 | loop fusion | flops 9830400 | bytes 32833736 | tf_op jit(solution)/shard_map/mul | solution.py:144
  645.1 14.0 %copy.105 = f32[10,256,5,256]{3,1,2,0:T(8,128)} copy(f32[10,256,5,256]{1,3,2,0:T(8,128)} %get-tuple-element.67) | data formatting | bytes 26214400 | tf_op jit(solution)/shard_map/jit(tril)/select_n | solution.py:13
  659.1 14.2 %copy.108 = f32[10,256,5,256]{3,1,2,0:T(8,128)} copy(f32[10,256,5,256]{1,3,2,0:T(8,128)} %get-tuple-element.66) | data formatting | bytes 26214400 | tf_op jit(solution)/shard_map/mul | solution.py:144
  673.4 10.4 %copy.109 = f32[2560,2,256]{2,1,0:T(2,128)} copy(f32[2560,2,256]{2,0,1:T(8,128)} %copy-done) | data formatting | bytes 10485760 | tf_op jit(solution)/shard_map/scatter | solution.py:119
  683.8 8.0 %reshape.409 = f32[10,256,512,1]{2,1,0,3:T(8,128)} reshape(f32[2560,2,256]{2,1,0:T(2,128)} %copy.109) | data formatting | bytes 10485760 | tf_op jit(solution)/shard_map/dot_general | solution.py:127
  691.8 2.0 dynamic-slice_bitcast_fusion
  693.8 30.4 %fusion.6 = f32[10,1,256,5,1,256]{5,2,3,0,4,1:T(8,128)S(1)} fusion(f32[10,256,5,256]{3,1,2,0:T(8,128)} %copy.105, f32[10,256,5,256]{3,1,2,0:T(8,128)} %copy.108, bf16[10,1,256,5,1,256]{2,5,3,0,4,1:T(8,128)(2,1)} %copy.103, f32[10,256,256]{2,1,0:T(8,128)S(1)} %dynamic-slice_bitcast_fusion, pred[5]{0:T(512)(128)(4,1)S(1)} %broadcast_compare_fusion.3, ...), kind=kOutput, calls=%fused_computation.17 | convolution fusion | flops 20158873600 | bytes 56426652 | tf_op jit(solution)/shard_map/dot_general | solution.py:127
  724.3 15.0 %copy.111 = f32[10,1,256,5,1,256]{5,4,3,2,1,0:T(1,128)} copy(f32[10,1,256,5,1,256]{5,2,3,0,4,1:T(8,128)S(1)} %fusion.6) | data formatting | bytes 26214400 | tf_op jit(solution)/shard_map/reshape | solution.py:151
  (120 shorter events, 17.5 us)
Async XLA Ops:
  13.0 31.0 %all-to-all-start = ((f32[4,1,64]{2,1,0:T(1,128)}), f32[4,1,64]{2,1,0:T(1,128)S(1)}, u32[]{:S(2)}, u32[]{:S(2)}) async-start(f32[4,1,64]{2,1,0:T(1,128)} %all_to_all.9), calls=%async_computation | async-start | bytes 4096 | tf_op jit(solution)/shard_map/all_to_all | solution.py:88
  17.3 1.3 slice-start
  18.6 1.2 copy-start.9
  44.0 12.3 %all-to-all-start.1 = ((f32[4,64,2,256]{3,2,1,0:T(2,128)}), f32[4,64,2,256]{3,2,1,0:T(2,128)S(1)}, u32[]{:S(2)}, u32[]{:S(2)}) async-start(f32[4,64,2,256]{3,2,1,0:T(2,128)} %bitcast.26), calls=%async_computation.1 | async-start | bytes 1048576 | tf_op jit(solution)/shard_map/all_to_all | solution.py:81
  47.5 301.8 %all-reduce.4.cloned.1.call-start = ((), (), s32[]{:S(2)}) async-start(), calls=%async_computation.2 | async-start | bytes 1572864 | tf_op jit(solution)/shard_map/psum | solution.py:104
  96.0 114.2 %collective-permute-start = (f32[2560,2,256]{0,2,1:T(8,128)}, f32[2560,2,256]{0,2,1:T(8,128)S(1)}, u32[]{:S(2)}, u32[]{:S(2)}) collective-permute-start(f32[2560,2,256]{0,2,1:T(8,128)} %copy.91), channel_id=1, source_target_pairs={{0,1},{1,0},{2,3},{3,2},{4,5},{5,4},{6,7},{7,6},{8,9},{9,8},{10,11... | collective-permute-start | bytes 15728648 | tf_op jit(solution)/shard_map/ppermute | solution.py:114
  216.0 141.9 %collective-permute-start.1 = (f32[2560,2,256]{0,2,1:T(8,128)}, f32[2560,2,256]{0,2,1:T(8,128)}, u32[]{:S(2)}, u32[]{:S(2)}) collective-permute-start(f32[2560,2,256]{0,2,1:T(8,128)} %add.191), channel_id=1, source_target_pairs={{0,2},{1,3},{2,0},{3,1},{4,6},{5,7},{6,4},{7,5},{8,10},{9,11},{10,... | collective-permute-start | bytes 15728648 | tf_op jit(solution)/shard_map/ppermute | solution.py:114
  219.7 9.5 %copy-start.12 = (s32[40,40]{1,0:T(8,128)S(1)}, s32[40,40]{1,0:T(8,128)}, u32[]{:S(2)}) copy-start(s32[40,40]{1,0:T(8,128)} %param.16) | copy-start | bytes 19204
  219.7 474.2 %all-reduce.6.cloned.1.call-start = ((), (), s32[]{:S(2)}) async-start(), calls=%async_computation.3 | async-start | bytes 5242880 | tf_op jit(solution)/shard_map/psum | solution.py:9
  349.3 3.2 copy-start.6
  365.3 227.2 %collective-permute-start.2 = (f32[2560,2,256]{0,2,1:T(8,128)}, f32[2560,2,256]{0,2,1:T(8,128)}, u32[]{:S(2)}, u32[]{:S(2)}) collective-permute-start(f32[2560,2,256]{0,2,1:T(8,128)} %add.192), channel_id=1, source_target_pairs={{0,4},{1,5},{2,6},{3,7},{4,0},{5,1},{6,2},{7,3},{8,12},{9,13},{10,... | collective-permute-start | bytes 15728648 | tf_op jit(solution)/shard_map/ppermute | solution.py:114
  597.7 2.4 copy-start.1
  600.0 1.5 copy-start.3
  608.2 4.4 copy-start.11
  613.9 1.1 copy-start.2
  620.1 1.3 copy-start.5
  621.4 2.4 copy-start.4
  624.1 1.0 copy-start.7
  624.1 1.0 copy-start.8
  625.2 2.4 copy-start
  632.8 0.8 copy-start.10
Sparse Core Ops, SparseCore 0:
  219.8 129.4 all-reduce.3
  633.0 58.6 all-reduce.5
